TPU v7x, 512 devices: a whole 4x4x16 slice. The times are simulated.
512 devices in a mesh: ref: 16 (over y_hi, x, core), dom: 32 (over y_lo, z).
Axes of the slice: x: 4, y: 4 (y_hi: 2, y_lo: 2; y = y_hi * 2 + y_lo), z: 16, core: 2. Of those that a mesh axis runs over, the one named last changes fastest.
Arguments:
- particles: bfloat16 [16384, 4096], P(('ref', 'dom'))
- inv_noise: float32 [16384], P(('ref', 'dom')), may hold values from 1 to 6
- candidates: int32 [16384, 8], P(('ref', 'dom')), may hold values from 0 to 127, as said below
- offsets: int32 [9, 2], replicated, may hold values from -2 to 2, as said below
- references: bfloat16 [128, 4096], P('ref')
Outputs:
- refreshed: bfloat16 [128, 4096], P('ref', 'dom')
- log_evidence: float32 [16384], P(('ref', 'dom'))
Inputs may be any that keep to these rules, and one draw needn't show every extreme that they name: `candidates`: each row names 8 different classes; class loads are uneven. `offsets`: 9 different shifts.
All inputs are finite; a program needn't handle non-finite values.
Results may differ from a plain program's by a relative error of at most 0.0038.
Values may be sent and summed in bfloat16 or wider, within the bound.
No kernel may reach another device: no remote copies, remote signals or barrier semaphores. Data moves between devices by JAX's collectives and lax.ppermute only.
A program may use at most 64 MiB of HBM per device.

v0:
```python
import jax
import jax.numpy as jnp
from jax import lax
from jax.sharding import PartitionSpec as P

SIDE = 64


def flat_roll(images, row_move, col_move):
    pixels = SIDE * SIDE
    moved = jnp.roll(images, row_move * SIDE, axis=1)
    col_mod = jnp.mod(col_move, SIDE)
    column = jnp.arange(pixels, dtype=jnp.int32) % SIDE
    inside = jnp.roll(moved, col_mod, axis=1)
    wrapped = jnp.roll(moved, col_mod - SIDE, axis=1)
    return jnp.where((column >= col_mod)[None, :], inside, wrapped)


def roll_set(images, offsets, sign):
    translated_image = []
    for shift_idx in range(offsets.shape[0]):
        translated_image.append(
            flat_roll(images, sign * offsets[shift_idx, 0], sign * offsets[shift_idx, 1])
        )
    return jnp.stack(translated_image, axis=1)


def per_device(particles, inv_noise, candidates, offsets, references):
    tile_size = references.shape[0]
    all_classes = tile_size * lax.axis_size("ref")
    stacked = roll_set(particles, offsets, -1)
    tile_rows = lax.all_gather(references, "ref", axis=0, tiled=True)
    tile_float = tile_rows.astype(jnp.float32)
    norms = jnp.sum(tile_float * tile_float, axis=1)
    translated_image = roll_set(tile_rows, offsets, 1)
    match_score = jnp.einsum(
        "vi,jti->vtj", particles, translated_image, preferred_element_type=jnp.float32
    )
    update = match_score - 0.5 * norms[None, None, :]
    score = inv_noise[:, None, None] * update
    classes = jnp.arange(all_classes, dtype=jnp.int32)
    permitted_mask = jnp.any(candidates[:, :, None] == classes[None, None, :], axis=1)
    masked = jnp.where(permitted_mask[:, None, :], score, -1e30)
    peak_val = jnp.max(masked, axis=(1, 2))
    denom_sum = jnp.sum(jnp.exp(masked - peak_val[:, None, None]), axis=(1, 2))
    evidence = peak_val + jnp.log(denom_sum)
    weight = jnp.where(
        permitted_mask[:, None, :], jnp.exp(masked - evidence[:, None, None]), 0.0
    ).astype(jnp.bfloat16)
    summed = lax.psum_scatter(
        jnp.einsum("psk,psq->kq", weight, stacked, preferred_element_type=jnp.float32),
        "ref",
        scatter_dimension=0,
        tiled=True,
    )
    shares = lax.psum_scatter(summed, "dom", scatter_dimension=1, tiled=True)
    row_power = lax.psum(jnp.sum(shares * shares, axis=1), "dom")
    refreshed = (shares / jnp.sqrt(row_power[:, None] / (SIDE * SIDE) + 1e-06)).astype(jnp.bfloat16)
    return (refreshed, evidence)


def solution(mesh):
    in_specs = (
        P(("ref", "dom"), None),
        P(("ref", "dom")),
        P(("ref", "dom"), None),
        P(),
        P("ref", None),
    )
    out_specs = (P("ref", "dom"), P(("ref", "dom")))
    return jax.shard_map(
        per_device, mesh=mesh, in_specs=in_specs, out_specs=out_specs, check_vma=False
    )
```

profile of v0, /device:TPU:2, one launch (start us, length us, event | category | flops | bytes accessed | tf_op | source)
XLA Modules:
  0.0 408.3 jit_solution(2184901198757844488)
XLA Ops:
  7.2 0.7 all-gather.2.cloned.1.call-update
  7.9 2.1 fusion.120
  39.1 1.0 constant_dynamic-update-slice_fusion.3
  40.1 1.0 constant_dynamic-update-slice_fusion.2
  41.5 1.0 constant_dynamic-slice_fusion.5
  42.5 0.6 fusion.91
  43.1 0.6 fusion.86
  43.7 0.6 fusion.81
  44.3 0.6 fusion.76
  44.9 0.6 fusion.71
  45.5 0.6 fusion.66
  46.1 0.6 fusion.61
  54.6 21.1 %all-gather.2.cloned.1.call-done = bf16[128,4096]{1,0:T(8,128)(2,1)} async-done(((bf16[8,4096]{1,0:T(8,128)(2,1)}), bf16[128,4096]{1,0:T(8,128)(2,1)}) %all-gather.2.cloned.1.call-update) | async-done | bytes 1048592 | tf_op jit(solution)/shard_map/all_gather | solution.py:32
  75.7 1.6 multiply_reduce_fusion
  77.3 1.3 constant_dynamic-update-slice_fusion.1
  78.8 5.6 %constant_dynamic-slice_fusion.9 = (bf16[128,4096]{1,0:T(8,128)(2,1)S(1)}, bf16[128,4096]{1,0:T(8,128)(2,1)S(1)}, bf16[128,4096]{1,0:T(8,128)(2,1)S(1)}, bf16[12...) fusion(bf16[128,8192]{1,0:T(8,128)(2,1)S(1)} %constant_dynamic-, ...), kind=kLoop, calls=%fused_computation.190 | loop fusion | bytes 18874404 | tf_op jit(solution)/shard_map/jit(_roll_dynamic)/dynamic_slice | solution.py:11
  84.3 1.7 fusion.46
  86.0 1.8 fusion.41
  87.8 1.8 fusion.36
  89.6 1.8 fusion.31
  91.4 1.8 fusion.26
  93.2 2.0 fusion.21
  95.2 1.8 fusion.16
  97.0 1.8 fusion.11
  98.8 1.8 fusion.6
  100.6 3.0 fusion.121
  103.8 2.2 convolution_bitcast_fusion
  106.1 93.1 %reduce-scatter.3.cloned.1.call-done = f32[8,4096]{1,0:T(8,128)} async-done(((f32[128,4096]{1,0:T(8,128)}), f32[8,4096]{1,0:T(8,128)}) %reduce-scatter.3.cloned.1.call-update) | async-done | bytes 131088 | tf_op jit(solution)/shard_map/reduce_scatter | solution.py:50
  199.2 139.1 %reduce-scatter.5.cloned.1.call-done = f32[8,128]{1,0:T(8,128)} async-done(((f32[8,4096]{1,0:T(8,128)}), f32[8,128]{1,0:T(8,128)}) %reduce-scatter.5.cloned.1.call-update) | async-done | bytes 4112 | tf_op jit(solution)/shard_map/reduce_scatter | solution.py:56
  338.3 0.8 multiply_reduce_fusion.1
  339.1 61.3 %psum.7 = f32[8]{0:T(128)S(1)} all-reduce(f32[8]{0:T(128)S(1)} %multiply_reduce_fusion.1), channel_id=1, replica_groups=mesh['ref'=16,'dom'=32] {'dom'}, use_global_device_ids=true, to_apply=%region_7.10 | all-reduce | flops 8 | bytes 64 | tf_op jit(solution)/shard_map/psum | solution.py:57
  400.4 1.3 divide_convert_fusion
  (34 shorter events, 2.0 us)
Async XLA Ops:
  7.2 68.6 %all-gather.2.cloned.1.call-start = ((), (), s32[]{:S(2)}) async-start(), calls=%async_computation.2 | async-start | bytes 1114112 | tf_op jit(solution)/shard_map/all_gather | solution.py:32
  7.9 191.3 %reduce-scatter.3.cloned.1.call-start = ((), (), s32[]{:S(2)}) async-start(), calls=%async_computation.3 | async-start | bytes 2228224 | tf_op jit(solution)/shard_map/reduce_scatter | solution.py:50
  43.1 10.0 %copy-start.2 = (s32[32,8]{0,1:T(8,128)S(1)}, s32[32,8]{0,1:T(8,128)}, u32[]{:S(2)}) copy-start(s32[32,8]{0,1:T(8,128)} %param.11) | copy-start | bytes 3076
  75.7 2.9 copy-start
  96.9 3.6 copy-start.1
  97.0 3.6 copy-start.3
  103.8 2.2 copy-start.4
  106.0 232.3 %reduce-scatter.5.cloned.1.call-start = ((), (), s32[]{:S(2)}) async-start(), calls=%async_computation.4 | async-start | bytes 135168 | tf_op jit(solution)/shard_map/reduce_scatter | solution.py:56
Sparse Core Ops, SparseCore 0:
  11.3 64.4 all-gather.1
  106.1 92.9 reduce-scatter.2
  202.0 136.3 reduce-scatter.4
where the time goes:
time: 409 us; the launch traced here: 408 us
  waiting for transfers between devices  254 us (62%)
  blocking collectives  61.3 us (15%)
  between operations  49.9 us (12%)
  other arithmetic  25.7 us (6%)
  local copies, waits for them, and re-layouts  12 us (3%)
  matrix products  5.16 us (1%)
    reduce_scatter x1, waiting for transfers between devices, per_device(): shares = lax.psum_scatter(summed, 'dom', scatter_dimension=1, tiled=True)  139 us
    reduce_scatter x1, waiting for transfers between devices, per_device(): lax.psum_scatter(jnp.einsum('psk,psq->kq', weight, stacked, preferred_ele...  93.1 us
    psum x1, blocking collectives, per_device(): row_power = lax.psum(jnp.sum(shares * shares, axis=1), 'dom')  61.3 us
    all_gather x1, waiting for transfers between devices, per_device(): tile_rows = lax.all_gather(references, 'ref', axis=0, tiled=True)  21.1 us
    unnamed x16, other arithmetic  19.2 us
  transfers between devices with their start and end apart: 3, of which 3 were waited for; matrix products, arithmetic and copies ran while one was open for 3% of the time, Pallas kernels for 0%

commit v1 on v0

--- a/solution.py
+++ b/solution.py
@@ -1,9 +1,18 @@
+import functools
 import jax
 import jax.numpy as jnp
 from jax import lax
 from jax.sharding import PartitionSpec as P
 
 SIDE = 64
+
+
+def kinds_bring(mine, mesh_dim):
+    mat_out = jax.lax.all_gather(mine, mesh_dim).sum(axis=0)
+    return mat_out
+
+
+register_patch_here = functools.partial(kinds_bring, mesh_dim="dom")
 
 
 def flat_roll(images, row_move, col_move):
@@ -54,7 +63,7 @@
         tiled=True,
     )
     shares = lax.psum_scatter(summed, "dom", scatter_dimension=1, tiled=True)
-    row_power = lax.psum(jnp.sum(shares * shares, axis=1), "dom")
+    row_power = register_patch_here(jnp.sum(shares * shares, axis=1))
     refreshed = (shares / jnp.sqrt(row_power[:, None] / (SIDE * SIDE) + 1e-06)).astype(jnp.bfloat16)
     return (refreshed, evidence)
 

time: 409 us -> 409 us (level)
  the two profiles are of different devices: /device:TPU:2 before, /device:TPU:6 now
where the time goes in v1:
time: 409 us
  waiting for transfers between devices  252 us (62%)
  blocking collectives  61.3 us (15%)
  between operations  50.3 us (12%)
  other arithmetic  25.8 us (6%)
  local copies, waits for them, and re-layouts  13.6 us (3%)
  matrix products  5.18 us (1%)
    reduce_scatter x1, waiting for transfers between devices, per_device(): shares = lax.psum_scatter(summed, 'dom', scatter_dimension=1, tiled=True)  137 us
    reduce_scatter x1, waiting for transfers between devices, per_device(): lax.psum_scatter(jnp.einsum('psk,psq->kq', weight, stacked, preferred_ele...  93.1 us
    unnamed x1, blocking collectives  61.3 us
    all_gather x1, waiting for transfers between devices, per_device(): tile_rows = lax.all_gather(references, 'ref', axis=0, tiled=True)  21.3 us
    unnamed x16, other arithmetic  19.2 us
  transfers between devices with their start and end apart: 3, of which 3 were waited for; matrix products, arithmetic and copies ran while one was open for 3% of the time, Pallas kernels for 0%

profile of v1, /device:TPU:6, one launch (start us, length us, event | category | flops | bytes accessed | tf_op | source)
XLA Modules:
  0.0 408.6 jit_solution(10187425489579379931)
XLA Ops:
  7.2 0.7 all-gather.3.cloned.1.call-update
  7.9 2.1 fusion.120
  38.9 1.0 constant_dynamic-update-slice_fusion.3
  39.9 1.0 constant_dynamic-update-slice_fusion.2
  41.3 1.0 constant_dynamic-slice_fusion.5
  42.3 0.6 fusion.91
  42.9 0.6 fusion.86
  43.5 0.6 fusion.81
  44.1 0.6 fusion.76
  44.7 0.6 fusion.71
  53.8 0.6 fusion.51
  54.4 21.3 %all-gather.3.cloned.1.call-done = bf16[128,4096]{1,0:T(8,128)(2,1)} async-done(((bf16[8,4096]{1,0:T(8,128)(2,1)}), bf16[128,4096]{1,0:T(8,128)(2,1)}) %all-gather.3.cloned.1.call-update) | async-done | bytes 1048592 | tf_op jit(solution)/shard_map/all_gather | solution.py:41
  75.7 1.6 multiply_reduce_fusion
  77.3 1.3 constant_dynamic-update-slice_fusion.1
  78.7 5.6 %constant_dynamic-slice_fusion.9 = (bf16[128,4096]{1,0:T(8,128)(2,1)S(1)}, bf16[128,4096]{1,0:T(8,128)(2,1)S(1)}, bf16[128,4096]{1,0:T(8,128)(2,1)S(1)}, bf16[12...) fusion(bf16[128,8192]{1,0:T(8,128)(2,1)S(1)} %constant_dynamic-, ...), kind=kLoop, calls=%fused_computation.190 | loop fusion | bytes 18874404 | tf_op jit(solution)/shard_map/jit(_roll_dynamic)/dynamic_slice | solution.py:20
  84.3 1.7 fusion.46
  86.0 1.8 fusion.41
  87.7 1.8 fusion.36
  89.5 1.8 fusion.31
  91.3 1.8 fusion.26
  93.1 2.0 fusion.21
  95.1 1.8 fusion.16
  96.9 1.8 fusion.11
  98.7 1.8 fusion.6
  100.5 3.0 fusion.121
  103.8 2.2 convolution_bitcast_fusion
  106.0 93.1 %reduce-scatter.3.cloned.1.call-done = f32[8,4096]{1,0:T(8,128)} async-done(((f32[128,4096]{1,0:T(8,128)}), f32[8,4096]{1,0:T(8,128)}) %reduce-scatter.3.cloned.1.call-update) | async-done | bytes 131088 | tf_op jit(solution)/shard_map/reduce_scatter | solution.py:59
  199.2 1.3 dynamic-slice
  201.1 137.2 %reduce-scatter.5.cloned.1.call-done = f32[8,128]{1,0:T(8,128)} async-done(((f32[8,4096]{1,0:T(8,128)}), f32[8,128]{1,0:T(8,128)}) %reduce-scatter.5.cloned.1.call-update) | async-done | bytes 4112 | tf_op jit(solution)/shard_map/reduce_scatter | solution.py:65
  338.3 0.8 multiply_reduce_fusion.1
  339.4 61.3 %all-reduce = f32[256]{0:T(256)S(1)} all-reduce(f32[256]{0:T(256)S(1)} %dynamic-update-slice), channel_id=2, replica_groups=mesh['ref'=16,'dom'=32] {'dom'}, use_global_device_ids=true, to_apply=%add | all-reduce | flops 256 | bytes 2048
  400.8 1.3 divide_convert_fusion
  (39 shorter events, 2.9 us)
Async XLA Ops:
  7.2 68.5 %all-gather.3.cloned.1.call-start = ((), (), s32[]{:S(2)}) async-start(), calls=%async_computation.2 | async-start | bytes 1114112 | tf_op jit(solution)/shard_map/all_gather | solution.py:41
  7.9 191.2 %reduce-scatter.3.cloned.1.call-start = ((), (), s32[]{:S(2)}) async-start(), calls=%async_computation.3 | async-start | bytes 2228224 | tf_op jit(solution)/shard_map/reduce_scatter | solution.py:59
  42.9 10.0 %copy-start.2 = (s32[32,8]{0,1:T(8,128)S(1)}, s32[32,8]{0,1:T(8,128)}, u32[]{:S(2)}) copy-start(s32[32,8]{0,1:T(8,128)} %param.11) | copy-start | bytes 3076
  75.7 2.9 copy-start
  96.9 3.6 copy-start.1
  96.9 3.6 copy-start.3
  103.8 2.2 copy-start.4
  106.0 232.3 %reduce-scatter.5.cloned.1.call-start = ((), (), s32[]{:S(2)}) async-start(), calls=%async_computation.4 | async-start | bytes 135168 | tf_op jit(solution)/shard_map/reduce_scatter | solution.py:65
Sparse Core Ops, SparseCore 0:
  11.3 64.3 all-gather.2
  106.1 92.9 reduce-scatter.2
  201.9 136.3 reduce-scatter.4
